TPU v7x, 32 devices: a whole 2x2x4 slice. The times are simulated.
32 devices in a mesh: section: 4 (over y, x), expert: 8 (over z, core).
Axes of the slice: x: 2, y: 2, z: 4, core: 2. Of those that a mesh axis runs over, the one named last changes fastest.
Arguments:
- tokens: bfloat16 [4, 2, 256, 2048], P('section', None, 'expert'), may hold values from -6 to 6
- routes: int32 [4, 2, 256, 2], P('section', None, 'expert'), may hold values from 0 to 3, all different within a row; in each aligned block of 32 rows (0 to 31, 32 to 63, ..., all dimensions but the last counted through in order) at most 24 rows name the same one
- combine_weights: float32 [4, 2, 256, 2], P('section', None, 'expert'), may hold values from 0.3 to 1
- norm_gain: float32 [4, 2048], P('section'), may hold values from 0.5 to 1.5
- gate_up: bfloat16 [4, 8, 2048, 768], P('section', 'expert'), may hold values from -0.125 to 0.125
- down: bfloat16 [4, 8, 384, 2048], P('section', 'expert'), may hold values from -0.21875 to 0.21875
Outputs:
- next_inputs: bfloat16 [4, 2, 256, 2048], P('section', None, 'expert')
Inputs may be any that keep to these rules, and one draw needn't show every extreme that they name: `routes`: each token names 2 different experts. Among the 32 tokens of one device in one section and micro-batch (aligned blocks of 32 rows) no expert is named more than 24 times.
All inputs are finite; a program needn't handle non-finite values.
Results may differ from a plain program's by a relative error of at most 0.0055.
Values may be sent and summed in bfloat16 or wider, within the bound.
No kernel may reach another device: no remote copies, remote signals or barrier semaphores. Data moves between devices by JAX's collectives and lax.ppermute only.
A program may use at most 64 MiB of HBM per device.

v0:
```python
import jax
import jax.numpy as jnp
from jax import lax
from jax.sharding import PartitionSpec as P

EPSILON = 1e-06


def from_behind(value, axis, steps):
    count = lax.axis_size(axis)
    pairs = [(source, (source + steps) % count) for source in range(count)]
    return lax.ppermute(value, axis, pairs)


def slot_codes(route_block, experts, capacity):
    flat = route_block.reshape(-1)
    onehot = (flat[:, None] == jnp.arange(experts, dtype=jnp.int32)[None, :]).astype(jnp.int32)
    before = jnp.cumsum(onehot, axis=0) - onehot
    slot = jnp.sum(before * onehot, axis=1)
    return (flat * capacity + slot).reshape(route_block.shape)


def normalize(block, gain):
    values = block.astype(jnp.float32)
    scale = lax.rsqrt(jnp.mean(values * values, axis=-1, keepdims=True) + EPSILON)
    return (values * scale * gain).astype(jnp.bfloat16)


def expert_half(block, weights_gu, weights_dn):
    shape = block.shape
    token_rows = block.reshape(-1, shape[-1])
    units = weights_dn.shape[0]
    joined = jnp.dot(token_rows, weights_gu, preferred_element_type=jnp.float32)
    hidden = (jax.nn.silu(joined[:, :units]) * joined[:, units:]).astype(jnp.bfloat16)
    partial_out = jnp.dot(hidden, weights_dn, preferred_element_type=jnp.float32).astype(
        jnp.bfloat16
    )
    return partial_out.reshape(shape)


def handoff(layer_out):
    return from_behind(layer_out, "section", 1)


def local(tokens, routes, combine_weights, norm_gain, gate_up, down):
    experts = lax.axis_size("expert") // 2
    tok_count = tokens.shape[2]
    width = tokens.shape[3]
    topk = routes.shape[3]
    capacity = 2 * ((3 * tok_count * topk + 4 * experts - 1) // (4 * experts))
    weights_gu = gate_up[0, 0]
    weights_dn = down[0, 0]
    gain = norm_gain[0]
    inputs = tokens[0]
    choices_in = routes[0]
    weights_in = combine_weights[0]
    pieces = []
    for position in range(inputs.shape[0]):
        section_x = inputs[position : position + 1]
        count = section_x.shape[0]
        normed = normalize(section_x, gain)
        codes = jax.vmap(lambda block: slot_codes(block, experts, capacity))(
            choices_in[position : position + 1]
        )
        lanes = jnp.arange(experts * capacity, dtype=jnp.int32)
        onehot = jnp.any(codes[..., None] == lanes, axis=2).astype(jnp.bfloat16)
        buffer = jnp.einsum("mtq,mtd->qmd", onehot, normed, preferred_element_type=jnp.float32)
        buffer = buffer.astype(jnp.bfloat16).reshape(experts, capacity, count, width)
        outgoing = jnp.repeat(buffer, 2, axis=0)
        incoming = lax.all_to_all(outgoing, "expert", split_axis=0, concat_axis=0, tiled=True)
        parts = expert_half(incoming, weights_gu, weights_dn)
        returned = lax.all_to_all(parts, "expert", split_axis=0, concat_axis=0, tiled=True)
        pairs = returned.reshape(experts, 2, capacity, count, width)
        results = (pairs[:, 0].astype(jnp.float32) + pairs[:, 1].astype(jnp.float32)).astype(
            jnp.bfloat16
        )
        table = jnp.swapaxes(results.reshape(experts * capacity, count, width), 0, 1)
        flat_codes = codes.reshape(count, tok_count * topk)
        picked = table[jnp.arange(count)[:, None], flat_codes].reshape(
            count, tok_count, topk, width
        )
        mixed = section_x.astype(jnp.float32) + jnp.sum(
            weights_in[position : position + 1][..., None] * picked.astype(jnp.float32), axis=2
        )
        finished_layer = mixed.astype(jnp.bfloat16)
        pieces.append(handoff(finished_layer))
    moved = jnp.concatenate(pieces, axis=0)
    return moved[None]


def solution(mesh):
    return jax.shard_map(
        local,
        mesh=mesh,
        in_specs=(
            P("section", None, "expert", None),
            P("section", None, "expert", None),
            P("section", None, "expert", None),
            P("section", None),
            P("section", "expert", None, None),
            P("section", "expert", None, None),
        ),
        out_specs=P("section", None, "expert", None),
        check_vma=False,
    )
```

profile of v0, /device:TPU:0, one launch (start us, length us, event | category | flops | bytes accessed | tf_op | source)
XLA Modules:
  0.0 130.0 jit_solution(14057331167735075358)
XLA Ops:
  0.0 0.0 copy-start
  0.0 0.8 broadcast_multiply_fusion.1
  0.9 0.1 copy.59
  0.9 0.1 eq.103
  1.0 0.1 fusion.34
  1.1 0.1 reduce_window_sum.18
  1.2 0.2 select_reduce_fusion
  1.4 0.1 reduce_sum.74
  1.5 0.1 copy.60
  1.6 0.1 copy.52
  1.7 0.1 eq.96
  1.8 0.1 fusion.35
  1.9 0.1 reduce_window_sum.17
  2.0 0.2 select_reduce_fusion.1
  2.2 0.1 reduce_sum.68
  2.3 0.1 copy.53
  2.4 1.1 fusion.12
  3.5 0.7 bitcast_add_fusion.1
  4.2 0.1 fusion.36
  4.3 0.0 copy-start.1
  4.3 0.0 copy-start.4
  4.3 1.3 convolution_convert_fusion.2
  5.6 1.0 broadcast_in_dim.12
  6.6 6.4 %all-to-all-start.2 = ((bf16[8,24,1,2048]{3,1,2,0:T(8,128)(2,1)}), bf16[8,24,1,2048]{3,1,2,0:T(8,128)(2,1)}, u32[]{:S(2)}, u32[]{:S(2)}) async-start(bf16[8,24,1,2048]{3,1,2,0:T(8,128)(2,1)} %bitcast.133), calls=%async_computation.2 | async-start | bytes 1572864 | tf_op jit(solution)/shard_map/all_to_all | solution.py:70
  13.0 0.0 copy-done.1
  13.0 0.0 copy-done.4
  13.0 1.1 convolution_convert_fusion.3
  14.1 20.0 %all-to-all-done.2 = bf16[8,24,1,2048]{3,1,2,0:T(8,128)(2,1)} async-done(((bf16[8,24,1,2048]{3,1,2,0:T(8,128)(2,1)}), bf16[8,24,1,2048]{3,1,2,0:T(8,128)(2,1)}, u32[]{:S(2)}, u32[]{:S(2)}) %all-to-all-start.2) | async-done | bytes 786464 | tf_op jit(solution)/shard_map/all_to_all | solution.py:70
  34.0 2.0 %broadcast_in_dim.10 = bf16[4,2,24,2048]{3,2,1,0:T(8,128)(2,1)} broadcast(bf16[4,24,2048]{2,1,0:T(8,128)(2,1)} %bitcast.135), dimensions={0,2,3} | broadcast | bytes 1179648 | tf_op jit(solution)/shard_map/broadcast_in_dim | solution.py:69
  36.0 4.2 %all-to-all-start = ((bf16[8,24,1,2048]{3,1,2,0:T(8,128)(2,1)}), bf16[8,24,1,2048]{3,1,2,0:T(8,128)(2,1)}, u32[]{:S(2)}, u32[]{:S(2)}) async-start(bf16[8,24,1,2048]{3,1,2,0:T(8,128)(2,1)} %bitcast.134), calls=%async_computation | async-start | bytes 1572864 | tf_op jit(solution)/shard_map/all_to_all | solution.py:70
  40.2 0.0 copy-done
  40.2 0.0 copy-start.6
  40.2 2.0 %fusion = f32[192,768]{1,0:T(8,128)S(1)} fusion(bf16[192,2048]{1,0:T(8,128)(2,1)} %bitcast.28, bf16[1,1,2048,768]{3,2,1,0:T(8,128)(2,1)S(1)} %copy-done), kind=kOutput, calls=%fused_computation.2 | convolution fusion | flops 603979776 | bytes 4521984 | tf_op jit(solution)/shard_map/dot_general | solution.py:33
  42.3 0.0 copy-done.6
  42.3 1.5 %convolution_convert_fusion = bf16[192,2048]{1,0:T(8,128)(2,1)} fusion(bf16[1,1,384,2048]{3,2,1,0:T(8,128)(2,1)S(1)} %copy-done.6, f32[192,768]{1,0:T(8,128)S(1)} %fusion), kind=kOutput, calls=%fused_computation.6 | convolution fusion | flops 302825472 | bytes 2949120 | tf_op jit(solution)/shard_map/dot_general | solution.py:35
  43.8 17.4 %all-to-all-done = bf16[8,24,1,2048]{3,1,2,0:T(8,128)(2,1)} async-done(((bf16[8,24,1,2048]{3,1,2,0:T(8,128)(2,1)}), bf16[8,24,1,2048]{3,1,2,0:T(8,128)(2,1)}, u32[]{:S(2)}, u32[]{:S(2)}) %all-to-all-start) | async-done | bytes 786464 | tf_op jit(solution)/shard_map/all_to_all | solution.py:70
  61.2 4.2 %all-to-all-start.3 = ((bf16[8,24,1,2048]{3,1,2,0:T(8,128)(2,1)}), bf16[8,24,1,2048]{3,1,2,0:T(8,128)(2,1)}, u32[]{:S(2)}, u32[]{:S(2)}) async-start(bf16[8,24,1,2048]{3,1,2,0:T(8,128)(2,1)} %bitcast.138), calls=%async_computation.3 | async-start | bytes 1572864 | tf_op jit(solution)/shard_map/all_to_all | solution.py:72
  65.4 0.1 copy.64
  65.5 0.1 mul.203
  65.6 0.0 copy-done.5
  65.6 0.0 copy-start.7
  65.6 2.0 %fusion.2 = f32[192,768]{1,0:T(8,128)S(1)} fusion(bf16[192,2048]{1,0:T(8,128)(2,1)} %bitcast.9, bf16[1,1,2048,768]{3,2,1,0:T(8,128)(2,1)S(1)} %copy-done), kind=kOutput, calls=%fused_computation.4 | convolution fusion | flops 603979776 | bytes 4521984 | tf_op jit(solution)/shard_map/dot_general | solution.py:33
  67.6 0.0 copy-done.7
  67.6 1.5 %convolution_convert_fusion.1 = bf16[192,2048]{1,0:T(8,128)(2,1)} fusion(bf16[1,1,384,2048]{3,2,1,0:T(8,128)(2,1)S(1)} %copy-done.7, f32[192,768]{1,0:T(8,128)S(1)} %fusion.2), kind=kOutput, calls=%fused_computation.7 | convolution fusion | flops 302825472 | bytes 2949120 | tf_op jit(solution)/shard_map/dot_general | solution.py:35
  69.1 17.2 %all-to-all-done.3 = bf16[8,24,1,2048]{3,1,2,0:T(8,128)(2,1)} async-done(((bf16[8,24,1,2048]{3,1,2,0:T(8,128)(2,1)}), bf16[8,24,1,2048]{3,1,2,0:T(8,128)(2,1)}, u32[]{:S(2)}, u32[]{:S(2)}) %all-to-all-start.3) | async-done | bytes 786464 | tf_op jit(solution)/shard_map/all_to_all | solution.py:72
  86.3 4.2 %all-to-all-start.1 = ((bf16[8,24,1,2048]{3,1,2,0:T(8,128)(2,1)}), bf16[8,24,1,2048]{3,1,2,0:T(8,128)(2,1)}, u32[]{:S(2)}, u32[]{:S(2)}) async-start(bf16[8,24,1,2048]{3,1,2,0:T(8,128)(2,1)} %bitcast.137), calls=%async_computation.1 | async-start | bytes 1572864 | tf_op jit(solution)/shard_map/all_to_all | solution.py:72
  90.5 0.7 copy.58
  91.2 0.1 copy.57
  91.3 0.1 mul.190
  91.4 0.7 copy.51
  92.2 1.2 add_convert_fusion
  93.4 2.1 %gather_fusion.1 = bf16[64,2048]{1,0:T(8,128)(2,1)} fusion(bf16[1,96,2048]{2,1,0:T(8,128)(2,1)S(1)} %bitcast.131, s32[64]{0:T(128)S(1)} %or_bitcast_fusion), kind=kCustom, calls=%fused_computation.1 | custom fusion | bytes 524800 | tf_op jit(solution)/shard_map/gather | solution.py:79
  95.5 2.1 %reshape.660 = f32[1,32,2,2048]{3,2,1,0:T(2,128)} reshape(bf16[64,2048]{1,0:T(8,128)(2,1)} %gather_fusion.1) | data formatting | bytes 786432 | tf_op jit(solution)/shard_map/convert_element_type | solution.py:83
  97.6 13.9 %all-to-all-done.1 = bf16[8,24,1,2048]{3,1,2,0:T(8,128)(2,1)} async-done(((bf16[8,24,1,2048]{3,1,2,0:T(8,128)(2,1)}), bf16[8,24,1,2048]{3,1,2,0:T(8,128)(2,1)}, u32[]{:S(2)}, u32[]{:S(2)}) %all-to-all-start.1) | async-done | bytes 786464 | tf_op jit(solution)/shard_map/all_to_all | solution.py:72
  111.5 1.2 add_convert_fusion.1
  112.7 2.1 %gather_fusion = bf16[64,2048]{1,0:T(8,128)(2,1)} fusion(bf16[1,96,2048]{2,1,0:T(8,128)(2,1)S(1)} %bitcast.132, s32[64]{0:T(128)S(1)} %or_bitcast_fusion.1), kind=kCustom, calls=%fused_computation | custom fusion | bytes 524800 | tf_op jit(solution)/shard_map/gather | solution.py:79
  114.8 2.1 %reshape.657 = f32[1,32,2,2048]{3,2,1,0:T(2,128)} reshape(bf16[64,2048]{1,0:T(8,128)(2,1)} %gather_fusion) | data formatting | bytes 786432 | tf_op jit(solution)/shard_map/convert_element_type | solution.py:83
  116.9 1.8 %multiply_reduce_fusion = f32[32,2048]{1,0:T(8,128)S(1)} fusion(f32[1,32,2,2048]{3,2,1,0:T(2,128)} %reshape.660, f32[32,2]{1,0:T(8,128)} %copy.58), kind=kLoop, calls=%fused_computation.14 | loop fusion | flops 196608 | bytes 786688 | tf_op jit(solution)/shard_map/reduce_sum | solution.py:82
  118.7 1.8 %multiply_reduce_fusion.1 = f32[32,2048]{1,0:T(8,128)S(1)} fusion(f32[1,32,2,2048]{3,2,1,0:T(2,128)} %reshape.657, f32[32,2]{1,0:T(8,128)S(1)} %copy-done.3), kind=kLoop, calls=%fused_computation.15 | loop fusion | flops 196608 | bytes 786688 | tf_op jit(solution)/shard_map/reduce_sum | solution.py:82
  120.6 1.5 %collective-permute-start = (bf16[1,32,2048]{2,1,0:T(8,128)(2,1)S(1)}, bf16[1,32,2048]{2,1,0:T(8,128)(2,1)S(1)}, u32[]{:S(2)}, u32[]{:S(2)}) collective-permute-start(bf16[1,32,2048]{2,1,0:T(8,128)(2,1)S(1)} %get-tuple-element.7), channel_id=1, source_target_pairs={{0,8},{8,16},{16,24},{24,0},{1,9},{9,17},{17,25},{25,1},{2,10},{10... | collective-permute-start | bytes 393224 | tf_op jit(solution)/shard_map/ppermute | solution.py:12
  122.1 1.5 %collective-permute-start.1 = (bf16[1,32,2048]{2,1,0:T(8,128)(2,1)S(1)}, bf16[1,32,2048]{2,1,0:T(8,128)(2,1)S(1)}, u32[]{:S(2)}, u32[]{:S(2)}) collective-permute-start(bf16[1,32,2048]{2,1,0:T(8,128)(2,1)S(1)} %get-tuple-element.8), channel_id=1, source_target_pairs={{0,8},{8,16},{16,24},{24,0},{1,9},{9,17},{17,25},{25,1},{2,10},{10... | collective-permute-start | bytes 393224 | tf_op jit(solution)/shard_map/ppermute | solution.py:12
  123.6 4.3 %collective-permute-done = bf16[1,32,2048]{2,1,0:T(8,128)(2,1)S(1)} collective-permute-done((bf16[1,32,2048]{2,1,0:T(8,128)(2,1)S(1)}, bf16[1,32,2048]{2,1,0:T(8,128)(2,1)S(1)}, u32[]{:S(2)}, u32[]{:S(2)}) %collective-permute-start) | collective-permute-done | bytes 131104 | tf_op jit(solution)/shard_map/ppermute | solution.py:12
  127.9 1.4 %collective-permute-done.1 = bf16[1,32,2048]{2,1,0:T(8,128)(2,1)S(1)} collective-permute-done((bf16[1,32,2048]{2,1,0:T(8,128)(2,1)S(1)}, bf16[1,32,2048]{2,1,0:T(8,128)(2,1)S(1)}, u32[]{:S(2)}, u32[]{:S(2)}) %collective-permute-start.1) | collective-permute-done | bytes 131104 | tf_op jit(solution)/shard_map/ppermute | solution.py:12
  129.3 0.7 maximum_bitcast_fusion
  (14 shorter events, 0.1 us)
Async XLA Ops:
  0.0 40.2 %copy-start = (bf16[1,1,2048,768]{3,2,1,0:T(8,128)(2,1)S(1)}, bf16[1,1,2048,768]{3,2,1,0:T(8,128)(2,1)}, u32[]{:S(2)}) copy-start(bf16[1,1,2048,768]{3,2,1,0:T(8,128)(2,1)} %param.10) | copy-start | bytes 9437188
  4.3 8.7 %copy-start.1 = (bf16[1,2,32,2048]{3,2,1,0:T(8,128)(2,1)S(1)}, bf16[1,2,32,2048]{3,2,1,0:T(8,128)(2,1)}, u32[]{:S(2)}) copy-start(bf16[1,2,32,2048]{3,2,1,0:T(8,128)(2,1)} %param.6) | copy-start | bytes 786436
  4.3 8.7 %copy-start.4 = (f32[1,2048]{1,0:T(1,128)S(1)}, f32[1,2048]{1,0:T(1,128)}, u32[]{:S(2)}) copy-start(f32[1,2048]{1,0:T(1,128)} %param.9) | copy-start | bytes 24580
  6.6 27.4 %all-to-all-start.2 = ((bf16[8,24,1,2048]{3,1,2,0:T(8,128)(2,1)}), bf16[8,24,1,2048]{3,1,2,0:T(8,128)(2,1)}, u32[]{:S(2)}, u32[]{:S(2)}) async-start(bf16[8,24,1,2048]{3,1,2,0:T(8,128)(2,1)} %bitcast.133), calls=%async_computation.2 | async-start | bytes 1572864 | tf_op jit(solution)/shard_map/all_to_all | solution.py:70
  36.0 25.2 %all-to-all-start = ((bf16[8,24,1,2048]{3,1,2,0:T(8,128)(2,1)}), bf16[8,24,1,2048]{3,1,2,0:T(8,128)(2,1)}, u32[]{:S(2)}, u32[]{:S(2)}) async-start(bf16[8,24,1,2048]{3,1,2,0:T(8,128)(2,1)} %bitcast.134), calls=%async_computation | async-start | bytes 1572864 | tf_op jit(solution)/shard_map/all_to_all | solution.py:70
  40.2 2.1 %copy-start.6 = (bf16[1,1,384,2048]{3,2,1,0:T(8,128)(2,1)S(1)}, bf16[1,1,384,2048]{3,2,1,0:T(8,128)(2,1)}, u32[]{:S(2)}) copy-start(bf16[1,1,384,2048]{3,2,1,0:T(8,128)(2,1)} %param.11) | copy-start | bytes 4718596
  43.8 21.8 %copy-start.5 = (f32[1,2,32,2]{2,3,1,0:T(2,128)S(1)}, f32[1,2,32,2]{2,3,1,0:T(2,128)}, u32[]{:S(2)}) copy-start(f32[1,2,32,2]{2,3,1,0:T(2,128)} %param.8) | copy-start | bytes 1540
  61.2 25.2 %all-to-all-start.3 = ((bf16[8,24,1,2048]{3,1,2,0:T(8,128)(2,1)}), bf16[8,24,1,2048]{3,1,2,0:T(8,128)(2,1)}, u32[]{:S(2)}, u32[]{:S(2)}) async-start(bf16[8,24,1,2048]{3,1,2,0:T(8,128)(2,1)} %bitcast.138), calls=%async_computation.3 | async-start | bytes 1572864 | tf_op jit(solution)/shard_map/all_to_all | solution.py:72
  65.6 2.0 %copy-start.7 = (bf16[1,1,384,2048]{3,2,1,0:T(8,128)(2,1)S(1)}, bf16[1,1,384,2048]{3,2,1,0:T(8,128)(2,1)}, u32[]{:S(2)}) copy-start(bf16[1,1,384,2048]{3,2,1,0:T(8,128)(2,1)} %param.11) | copy-start | bytes 4718596
  86.3 25.2 %all-to-all-start.1 = ((bf16[8,24,1,2048]{3,1,2,0:T(8,128)(2,1)}), bf16[8,24,1,2048]{3,1,2,0:T(8,128)(2,1)}, u32[]{:S(2)}, u32[]{:S(2)}) async-start(bf16[8,24,1,2048]{3,1,2,0:T(8,128)(2,1)} %bitcast.137), calls=%async_computation.1 | async-start | bytes 1572864 | tf_op jit(solution)/shard_map/all_to_all | solution.py:72
  114.8 3.9 %copy-start.3 = (f32[32,2]{1,0:T(8,128)S(1)}, f32[32,2]{1,0:T(8,128)}, u32[]{:S(2)}) copy-start(f32[32,2]{1,0:T(8,128)} %copy.51) | copy-start | bytes 772
  114.8 5.7 %copy-start.2 = (bf16[1,2,32,2048]{3,2,1,0:T(8,128)(2,1)S(1)}, bf16[1,2,32,2048]{3,2,1,0:T(8,128)(2,1)}, u32[]{:S(2)}) copy-start(bf16[1,2,32,2048]{3,2,1,0:T(8,128)(2,1)} %param.6) | copy-start | bytes 786436
  120.6 7.3 %collective-permute-start = (bf16[1,32,2048]{2,1,0:T(8,128)(2,1)S(1)}, bf16[1,32,2048]{2,1,0:T(8,128)(2,1)S(1)}, u32[]{:S(2)}, u32[]{:S(2)}) collective-permute-start(bf16[1,32,2048]{2,1,0:T(8,128)(2,1)S(1)} %get-tuple-element.7), channel_id=1, source_target_pairs={{0,8},{8,16},{16,24},{24,0},{1,9},{9,17},{17,25},{25,1},{2,10},{10... | collective-permute-start | bytes 393224 | tf_op jit(solution)/shard_map/ppermute | solution.py:12
  122.1 7.2 %collective-permute-start.1 = (bf16[1,32,2048]{2,1,0:T(8,128)(2,1)S(1)}, bf16[1,32,2048]{2,1,0:T(8,128)(2,1)S(1)}, u32[]{:S(2)}, u32[]{:S(2)}) collective-permute-start(bf16[1,32,2048]{2,1,0:T(8,128)(2,1)S(1)} %get-tuple-element.8), channel_id=1, source_target_pairs={{0,8},{8,16},{16,24},{24,0},{1,9},{9,17},{17,25},{25,1},{2,10},{10... | collective-permute-start | bytes 393224 | tf_op jit(solution)/shard_map/ppermute | solution.py:12
where the time goes:
time: 131 us; the launch traced here: 130 us
  waiting for transfers between devices  74.1 us (57%)
  starting transfers between devices  22 us (17%)
  local copies, waits for them, and re-layouts  14 us (11%)
  other arithmetic  10.3 us (8%)
  matrix products  9.4 us (7%)
    all_to_all x2, waiting for transfers between devices, local(): lax.all_to_all(outgoing, 'expert', split_axis=0, concat_axis=0, tiled=True)  37.3 us
    all_to_all x2, waiting for transfers between devices, local(): lax.all_to_all(parts, 'expert', split_axis=0, concat_axis=0, tiled=True)  31.1 us
    all_to_all x2, starting transfers between devices, local(): lax.all_to_all(outgoing, 'expert', split_axis=0, concat_axis=0, tiled=True)  10.6 us
    all_to_all x2, starting transfers between devices, local(): lax.all_to_all(parts, 'expert', split_axis=0, concat_axis=0, tiled=True)  8.4 us
    ppermute x2, waiting for transfers between devices, from_behind(): return lax.ppermute(value, axis, pairs)  5.67 us
    gather x2, local copies, waits for them, and re-layouts, local(): table[jnp.arange(count)[:, None], flat_codes]  4.22 us
    convert_element_type x2, local copies, waits for them, and re-layouts, local(): picked.astype(jnp.float32)  4.21 us
    dot_general x2, matrix products, expert_half(): joined = jnp.dot(token_rows, weights_gu, preferred_element_type=jnp.float32)  4.06 us
  transfers between devices with their start and end apart: 6, of which 6 were waited for; matrix products, arithmetic and copies ran while one was open for 12% of the time, Pallas kernels for 0%

commit v1 on v0

--- a/solution.py
+++ b/solution.py
@@ -1,9 +1,40 @@
+import functools
 import jax
 import jax.numpy as jnp
 from jax import lax
 from jax.sharding import PartitionSpec as P
 
 EPSILON = 1e-06
+
+
+def thing_remake(sheet, chip_axis):
+    item_now = lax.axis_index(chip_axis)
+    heard = lax.axis_size(chip_axis)
+    n_now, taken_in = (heard, item_now)
+    ready = sheet.shape[0] // n_now
+    odd = list(sheet.shape)
+    odd[0] = ready
+    r2 = odd[0]
+    odd[0] = r2 * n_now
+    j = 0
+    field_out = jnp.zeros(odd, sheet.dtype)
+    while j < n_now:
+        everything = lax.dynamic_slice_in_dim(sheet, (taken_in ^ j) * ready, ready, axis=0)
+        if j:
+            grid = []
+            dev_j = 0
+            while dev_j < n_now:
+                grid.append((dev_j, dev_j ^ j))
+                dev_j = dev_j + 1
+            everything = lax.ppermute(everything, axis_name=chip_axis, perm=grid)
+        field_out = lax.dynamic_update_slice_in_dim(
+            field_out, everything, (taken_in ^ j) * r2, axis=0
+        )
+        j = j + 1
+    return field_out
+
+
+close_leaf = functools.partial(thing_remake, chip_axis="expert")
 
 
 def from_behind(value, axis, steps):
@@ -69,7 +100,7 @@
         outgoing = jnp.repeat(buffer, 2, axis=0)
         incoming = lax.all_to_all(outgoing, "expert", split_axis=0, concat_axis=0, tiled=True)
         parts = expert_half(incoming, weights_gu, weights_dn)
-        returned = lax.all_to_all(parts, "expert", split_axis=0, concat_axis=0, tiled=True)
+        returned = close_leaf(parts)
         pairs = returned.reshape(experts, 2, capacity, count, width)
         results = (pairs[:, 0].astype(jnp.float32) + pairs[:, 1].astype(jnp.float32)).astype(
             jnp.bfloat16

time: 131 us -> 122 us (0.931)
  waiting for transfers between devices: 74.1 us -> 41.8 us
  local copies, waits for them, and re-layouts: 14 us -> 31.8 us
  starting transfers between devices: 22 us -> 29.9 us
  matrix products: 9.4 us -> 7.62 us
    all_to_all x2 -> x0, waiting for transfers between devices: 31.1 us -> none  [local(): lax.all_to_all(parts, 'expert', split_axis=0, concat_axis=0, tiled=True)]
    ppermute x0 -> x14, starting transfers between devices: none -> 16.3 us  [thing_remake(): everything = lax.ppermute(everything, axis_name=chip_axis, perm=grid)]
    dynamic_update_slice x0 -> x14, local copies, waits for them, and re-layouts: none -> 14.3 us  [thing_remake(): lax.dynamic_update_slice_in_dim(field_out, everything, (taken_in ^ j) * r...]
    all_to_all x2 -> x0, starting transfers between devices: 8.4 us -> none  [local(): lax.all_to_all(parts, 'expert', split_axis=0, concat_axis=0, tiled=True)]
    all_to_all x2, waiting for transfers between devices: 37.3 us -> 30.5 us  [local(): lax.all_to_all(outgoing, 'expert', split_axis=0, concat_axis=0, tiled=True)]
    ppermute x0 -> x14, waiting for transfers between devices: none -> 5.03 us  [thing_remake(): everything = lax.ppermute(everything, axis_name=chip_axis, perm=grid)]
    another operation x0 -> x2, local copies, waits for them, and re-layouts: none -> 1.94 us
    dot_general x2, matrix products: 2.99 us -> 1.19 us  [expert_half(): jnp.dot(hidden, weights_dn, preferred_element_type=jnp.float32)]
  transfers between devices with their start and end apart: 6 -> 18, of which waited for: 6 -> 5; matrix products, arithmetic and copies ran while one was open for 12% -> 24% of each run, Pallas kernels for 0% -> 0%
where the time goes in v1:
time: 122 us
  waiting for transfers between devices  41.8 us (34%)
  local copies, waits for them, and re-layouts  31.8 us (26%)
  starting transfers between devices  29.9 us (25%)
  other arithmetic  10.3 us (8%)
  matrix products  7.62 us (6%)
    all_to_all x2, waiting for transfers between devices, local(): lax.all_to_all(outgoing, 'expert', split_axis=0, concat_axis=0, tiled=True)  30.5 us
    ppermute x14, starting transfers between devices, thing_remake(): everything = lax.ppermute(everything, axis_name=chip_axis, perm=grid)  16.3 us
    dynamic_update_slice x14, local copies, waits for them, and re-layouts, thing_remake(): lax.dynamic_update_slice_in_dim(field_out, everything, (taken_in ^ j) * r...  14.3 us
    all_to_all x2, starting transfers between devices, local(): lax.all_to_all(outgoing, 'expert', split_axis=0, concat_axis=0, tiled=True)  10.6 us
    ppermute x2, waiting for transfers between devices, from_behind(): return lax.ppermute(value, axis, pairs)  6.25 us
    ppermute x14, waiting for transfers between devices, thing_remake(): everything = lax.ppermute(everything, axis_name=chip_axis, perm=grid)  5.03 us
    convert_element_type x2, local copies, waits for them, and re-layouts, local(): picked.astype(jnp.float32)  4.23 us
    gather x2, local copies, waits for them, and re-layouts, local(): table[jnp.arange(count)[:, None], flat_codes]  4.22 us
  transfers between devices with their start and end apart: 18, of which 5 were waited for; matrix products, arithmetic and copies ran while one was open for 24% of the time, Pallas kernels for 0%

profile of v1, /device:TPU:0, one launch (start us, length us, event | category | flops | bytes accessed | tf_op | source)
XLA Modules:
  0.0 121.7 jit_solution(5265029174641017672)
XLA Ops:
  0.0 0.8 broadcast_multiply_fusion.1
  1.2 0.2 select_reduce_fusion
  1.7 0.1 eq.96
  2.0 0.2 select_reduce_fusion.1
  2.4 1.1 fusion.12
  3.5 0.7 bitcast_add_fusion.1
  4.3 1.3 %convolution_convert_fusion.2 = bf16[2048,96]{0,1:T(8,128)(2,1)S(1)} fusion(pred[32,96]{1,0:T(8,128)(4,1)S(1)} %get-tuple-element.36, f32[32]{0:T(128)S(1)} %get-tuple-element.37, f32[2048]{0:T(1024)} %bitcast.119, bf16[1,2,32,2048]{3,2,1,0:T(8,128)(2,1)} %param.6), kind=kOutput, calls=%fused_computation.8 | convolution fusion | flops 13041664 | bytes 535680 | tf_op jit(solution)/shard_map/mtq,mtd->qmd/dot_general | solution.py:98
  5.6 1.0 broadcast_in_dim.12
  6.6 6.4 %all-to-all-start.1 = ((bf16[8,24,1,2048]{3,1,2,0:T(8,128)(2,1)}), bf16[8,24,1,2048]{3,1,2,0:T(8,128)(2,1)}, u32[]{:S(2)}, u32[]{:S(2)}) async-start(bf16[8,24,1,2048]{3,1,2,0:T(8,128)(2,1)} %bitcast.114), calls=%async_computation.1 | async-start | bytes 1572864 | tf_op jit(solution)/shard_map/all_to_all | solution.py:101
  13.2 0.1 mul.203
  13.4 1.1 convolution_convert_fusion.3
  14.5 19.5 %all-to-all-done.1 = bf16[8,24,1,2048]{3,1,2,0:T(8,128)(2,1)} async-done(((bf16[8,24,1,2048]{3,1,2,0:T(8,128)(2,1)}), bf16[8,24,1,2048]{3,1,2,0:T(8,128)(2,1)}, u32[]{:S(2)}, u32[]{:S(2)}) %all-to-all-start.1) | async-done | bytes 786464 | tf_op jit(solution)/shard_map/all_to_all | solution.py:101
  34.0 2.0 %broadcast_in_dim.10 = bf16[4,2,24,2048]{3,2,1,0:T(8,128)(2,1)} broadcast(bf16[4,24,2048]{2,1,0:T(8,128)(2,1)} %bitcast.115), dimensions={0,2,3} | broadcast | bytes 1179648 | tf_op jit(solution)/shard_map/broadcast_in_dim | solution.py:100
  36.0 4.2 %all-to-all-start = ((bf16[8,24,1,2048]{3,1,2,0:T(8,128)(2,1)}), bf16[8,24,1,2048]{3,1,2,0:T(8,128)(2,1)}, u32[]{:S(2)}, u32[]{:S(2)}) async-start(bf16[8,24,1,2048]{3,1,2,0:T(8,128)(2,1)} %bitcast.113), calls=%async_computation | async-start | bytes 1572864 | tf_op jit(solution)/shard_map/all_to_all | solution.py:101
  40.3 0.7 copy.41
  40.9 0.7 copy.37
  41.7 2.0 %fusion = f32[192,768]{1,0:T(8,128)S(1)} fusion(bf16[192,2048]{1,0:T(8,128)(2,1)} %bitcast.27, bf16[1,1,2048,768]{3,2,1,0:T(8,128)(2,1)S(1)} %copy-done), kind=kOutput, calls=%fused_computation.2 | convolution fusion | flops 603979776 | bytes 4521984 | tf_op jit(solution)/shard_map/dot_general | solution.py:64
  43.7 0.6 convolution_convert_fusion
  44.3 1.0 broadcast.285.clone.1
  45.3 0.8 constant_dynamic-slice_fusion
  46.1 0.4 collective-permute-start.8
  46.4 1.6 %collective-permute-start.9 = (bf16[1,24,1,2048]{3,1,0,2:T(8,128)(2,1)}, bf16[1,24,1,2048]{3,1,0,2:T(8,128)(2,1)}, u32[]{:S(2)}, u32[]{:S(2)}) collective-permute-start(bf16[1,24,1,2048]{3,1,0,2:T(8,128)(2,1)} %get-tuple-element.20), channel_id=1, source_target_pairs={{0,2},{1,3},{2,0},{3,1},{4,6},{5,7},{6,4},{7,5},{8,10},{9,11},{10,... | collective-permute-start | bytes 294920 | tf_op jit(solution)/shard_map/ppermute | solution.py:29
  48.1 2.7 %collective-permute-start.11 = (bf16[1,24,1,2048]{3,1,0,2:T(8,128)(2,1)S(1)}, bf16[1,24,1,2048]{3,1,0,2:T(8,128)(2,1)}, u32[]{:S(2)}, u32[]{:S(2)}) collective-permute-start(bf16[1,24,1,2048]{3,1,0,2:T(8,128)(2,1)S(1)} %get-tuple-element.18), channel_id=1, source_target_pairs={{0,4},{1,5},{2,6},{3,7},{4,0},{5,1},{6,2},{7,3},{8,12},{9,13},{10,... | collective-permute-start | bytes 294920 | tf_op jit(solution)/shard_map/ppermute | solution.py:29
  50.8 11.0 %all-to-all-done = bf16[8,24,1,2048]{3,1,2,0:T(8,128)(2,1)} async-done(((bf16[8,24,1,2048]{3,1,2,0:T(8,128)(2,1)}), bf16[8,24,1,2048]{3,1,2,0:T(8,128)(2,1)}, u32[]{:S(2)}, u32[]{:S(2)}) %all-to-all-start) | async-done | bytes 786464 | tf_op jit(solution)/shard_map/all_to_all | solution.py:101
  61.9 2.0 %fusion.2 = f32[192,768]{1,0:T(8,128)S(1)} fusion(bf16[192,2048]{1,0:T(8,128)(2,1)} %bitcast.9, bf16[1,1,2048,768]{3,2,1,0:T(8,128)(2,1)S(1)} %copy-done), kind=kOutput, calls=%fused_computation.4 | convolution fusion | flops 603979776 | bytes 4521984 | tf_op jit(solution)/shard_map/dot_general | solution.py:64
  63.9 0.6 convolution_convert_fusion.1
  64.5 1.0 broadcast.285.clone
  65.5 0.7 constant_dynamic-slice_fusion.7
  66.2 0.9 collective-permute-start.13
  67.1 1.5 %constant_dynamic-update-slice_fusion.5 = bf16[8,24,1,2048]{3,1,0,2:T(8,128)(2,1)} fusion(bf16[8,24,1,2048]{3,1,0,2:T(8,128)(2,1)} %get-tuple-element.22, bf16[1,24,1,2048]{3,1,0,2:T(8,128)(2,1)} %collective-permute-done.8, s32[]{:T(128)S(6)} %select_n.73), kind=kLoop, calls=%fused_computation.70 | loop fusion | bytes 196612 | tf_op jit(solution)/shard_map/dynamic_update_slice | solution.py:30
  68.7 1.1 collective-permute-start.14
  69.8 1.5 %constant_dynamic-update-slice_fusion.4 = bf16[8,24,1,2048]{3,1,0,2:T(8,128)(2,1)} fusion(bf16[8,24,1,2048]{3,1,0,2:T(8,128)(2,1)} %constant_dynamic-update-slice_fusion.5, bf16[1,24,1,2048]{3,1,0,2:T(8,128)(2,1)} %collective-permute-done.9, s32[]{:T(128)S(6)} %select_n.74), kind=kLoop, calls=%fused_computation.68 | loop fusion | bytes 196612 | tf_op jit(solution)/shard_map/dynamic_update_slice | solution.py:30
  71.3 1.9 %collective-permute-start = (bf16[1,24,1,2048]{3,1,0,2:T(8,128)(2,1)S(1)}, bf16[1,24,1,2048]{3,1,0,2:T(8,128)(2,1)S(1)}, u32[]{:S(2)}, u32[]{:S(2)}) collective-permute-start(bf16[1,24,1,2048]{3,1,0,2:T(8,128)(2,1)S(1)} %get-tuple-element.13), channel_id=1, source_target_pairs={{0,1},{1,0},{2,3},{3,2},{4,5},{5,4},{6,7},{7,6},{8,9},{9,8},{10,11... | collective-permute-start | bytes 294920 | tf_op jit(solution)/shard_map/ppermute | solution.py:29
  73.2 1.5 %constant_dynamic-update-slice_fusion.3 = bf16[8,24,1,2048]{3,1,0,2:T(8,128)(2,1)} fusion(bf16[8,24,1,2048]{3,1,0,2:T(8,128)(2,1)} %constant_dynamic-update-slice_fusion.4, bf16[1,24,1,2048]{3,1,0,2:T(8,128)(2,1)} %collective-permute-done.10, s32[]{:T(128)S(6)} %select_n.75), kind=kLoop, calls=%fused_computation.66 | loop fusion | bytes 196612 | tf_op jit(solution)/shard_map/dynamic_update_slice | solution.py:30
  74.8 1.5 %constant_dynamic-update-slice_fusion.2 = bf16[8,24,1,2048]{3,1,0,2:T(8,128)(2,1)} fusion(bf16[8,24,1,2048]{3,1,0,2:T(8,128)(2,1)} %constant_dynamic-update-slice_fusion.3, bf16[1,24,1,2048]{3,1,0,2:T(8,128)(2,1)} %collective-permute-done.11, s32[]{:T(128)S(6)} %select_n.76), kind=kLoop, calls=%fused_computation.64 | loop fusion | bytes 196612 | tf_op jit(solution)/shard_map/dynamic_update_slice | solution.py:30
  76.3 1.3 %collective-permute-start.2 = (bf16[1,24,1,2048]{3,1,0,2:T(8,128)(2,1)S(1)}, bf16[1,24,1,2048]{3,1,0,2:T(8,128)(2,1)S(1)}, u32[]{:S(2)}, u32[]{:S(2)}) collective-permute-start(bf16[1,24,1,2048]{3,1,0,2:T(8,128)(2,1)S(1)} %get-tuple-element.11), channel_id=1, source_target_pairs={{0,3},{1,2},{2,1},{3,0},{4,7},{5,6},{6,5},{7,4},{8,11},{9,10},{10,... | collective-permute-start | bytes 294920 | tf_op jit(solution)/shard_map/ppermute | solution.py:29
  77.7 1.5 %constant_dynamic-update-slice_fusion.1 = bf16[8,24,1,2048]{3,1,0,2:T(8,128)(2,1)} fusion(bf16[8,24,1,2048]{3,1,0,2:T(8,128)(2,1)} %constant_dynamic-update-slice_fusion.2, bf16[1,24,1,2048]{3,1,0,2:T(8,128)(2,1)} %collective-permute-done.12, s32[]{:T(128)S(6)} %select_n.77), kind=kLoop, calls=%fused_computation.62 | loop fusion | bytes 196612 | tf_op jit(solution)/shard_map/dynamic_update_slice | solution.py:30
  79.2 0.1 collective-permute-start.3
  79.3 0.6 constant_dynamic-update-slice_fusion
  80.0 2.9 %collective-permute-start.4 = (bf16[1,24,1,2048]{3,1,0,2:T(8,128)(2,1)S(1)}, bf16[1,24,1,2048]{3,1,0,2:T(8,128)(2,1)S(1)}, u32[]{:S(2)}, u32[]{:S(2)}) collective-permute-start(bf16[1,24,1,2048]{3,1,0,2:T(8,128)(2,1)S(1)} %get-tuple-element.9), channel_id=1, source_target_pairs={{0,5},{1,4},{2,7},{3,6},{4,1},{5,0},{6,3},{7,2},{8,13},{9,12},{10,... | collective-permute-start | bytes 294920 | tf_op jit(solution)/shard_map/ppermute | solution.py:29
  82.9 0.6 constant_dynamic-update-slice_fusion.13
  83.5 1.2 add_convert_fusion
  84.8 1.0 collective-permute-start.5
  85.7 0.6 constant_dynamic-update-slice_fusion.12
  86.4 2.2 %collective-permute-start.6 = (bf16[1,24,1,2048]{3,1,0,2:T(8,128)(2,1)}, bf16[1,24,1,2048]{3,1,0,2:T(8,128)(2,1)}, u32[]{:S(2)}, u32[]{:S(2)}) collective-permute-start(bf16[1,24,1,2048]{3,1,0,2:T(8,128)(2,1)} %get-tuple-element.7), channel_id=1, source_target_pairs={{0,7},{1,6},{2,5},{3,4},{4,3},{5,2},{6,1},{7,0},{8,15},{9,14},{10,... | collective-permute-start | bytes 294920 | tf_op jit(solution)/shard_map/ppermute | solution.py:29
  88.6 0.6 constant_dynamic-update-slice_fusion.11
  89.3 0.6 constant_dynamic-update-slice_fusion.10
  89.9 0.6 constant_dynamic-update-slice_fusion.9
  90.5 5.0 %collective-permute-done.4 = bf16[1,24,1,2048]{3,1,0,2:T(8,128)(2,1)S(1)} collective-permute-done((bf16[1,24,1,2048]{3,1,0,2:T(8,128)(2,1)S(1)}, bf16[1,24,1,2048]{3,1,0,2:T(8,128)(2,1)S(1)}, u32[]{:S(2)}, u32[]{:S(2)}) %collective-permute-start.4) | collective-permute-done | bytes 98336 | tf_op jit(solution)/shard_map/ppermute | solution.py:29
  95.5 0.6 constant_dynamic-update-slice_fusion.8
  96.2 0.6 constant_dynamic-update-slice_fusion.7
  96.8 2.1 %gather_fusion.1 = bf16[64,2048]{1,0:T(8,128)(2,1)} fusion(bf16[1,96,2048]{2,1,0:T(8,128)(2,1)S(1)} %bitcast.111, s32[64]{0:T(128)S(1)} %or_bitcast_fusion), kind=kCustom, calls=%fused_computation.1 | custom fusion | bytes 524800 | tf_op jit(solution)/shard_map/gather | solution.py:110
  98.9 2.1 %reshape.660 = f32[1,32,2,2048]{3,2,1,0:T(2,128)} reshape(bf16[64,2048]{1,0:T(8,128)(2,1)} %gather_fusion.1) | data formatting | bytes 786432 | tf_op jit(solution)/shard_map/convert_element_type | solution.py:114
  101.0 1.5 %constant_dynamic-update-slice_fusion.6 = bf16[8,24,1,2048]{3,1,0,2:T(8,128)(2,1)} fusion(bf16[8,24,1,2048]{3,1,0,2:T(8,128)(2,1)} %constant_dynamic-update-slice_fusion.7, bf16[1,24,1,2048]{3,1,0,2:T(8,128)(2,1)} %collective-permute-done.6, s32[]{:T(128)S(6)} %select_n.79), kind=kLoop, calls=%fused_computation.72 | loop fusion | bytes 196612 | tf_op jit(solution)/shard_map/dynamic_update_slice | solution.py:30
  102.6 1.2 add_convert_fusion.1
  103.8 2.1 %gather_fusion = bf16[64,2048]{1,0:T(8,128)(2,1)} fusion(bf16[1,96,2048]{2,1,0:T(8,128)(2,1)S(1)} %bitcast.112, s32[64]{0:T(128)S(1)} %or_bitcast_fusion.1), kind=kCustom, calls=%fused_computation | custom fusion | bytes 524800 | tf_op jit(solution)/shard_map/gather | solution.py:110
  105.9 2.1 %reshape.657 = f32[1,32,2,2048]{3,2,1,0:T(2,128)} reshape(bf16[64,2048]{1,0:T(8,128)(2,1)} %gather_fusion) | data formatting | bytes 786432 | tf_op jit(solution)/shard_map/convert_element_type | solution.py:114
  108.0 1.8 %multiply_reduce_fusion = f32[32,2048]{1,0:T(8,128)S(1)} fusion(f32[1,32,2,2048]{3,2,1,0:T(2,128)} %reshape.660, f32[32,2]{1,0:T(8,128)} %copy.41), kind=kLoop, calls=%fused_computation.14 | loop fusion | flops 196608 | bytes 786688 | tf_op jit(solution)/shard_map/reduce_sum | solution.py:113
  109.8 1.8 %multiply_reduce_fusion.1 = f32[32,2048]{1,0:T(8,128)S(1)} fusion(f32[1,32,2,2048]{3,2,1,0:T(2,128)} %reshape.657, f32[32,2]{1,0:T(8,128)S(1)} %copy-done.3), kind=kLoop, calls=%fused_computation.15 | loop fusion | flops 196608 | bytes 786688 | tf_op jit(solution)/shard_map/reduce_sum | solution.py:113
  111.7 1.5 %collective-permute-start.15 = (bf16[1,32,2048]{2,1,0:T(8,128)(2,1)S(1)}, bf16[1,32,2048]{2,1,0:T(8,128)(2,1)S(1)}, u32[]{:S(2)}, u32[]{:S(2)}) collective-permute-start(bf16[1,32,2048]{2,1,0:T(8,128)(2,1)S(1)} %get-tuple-element.24), channel_id=1, source_target_pairs={{0,8},{8,16},{16,24},{24,0},{1,9},{9,17},{17,25},{25,1},{2,10},{10... | collective-permute-start | bytes 393224 | tf_op jit(solution)/shard_map/ppermute | solution.py:43
  113.2 1.5 %collective-permute-start.7 = (bf16[1,32,2048]{2,1,0:T(8,128)(2,1)S(1)}, bf16[1,32,2048]{2,1,0:T(8,128)(2,1)S(1)}, u32[]{:S(2)}, u32[]{:S(2)}) collective-permute-start(bf16[1,32,2048]{2,1,0:T(8,128)(2,1)S(1)} %get-tuple-element.23), channel_id=1, source_target_pairs={{0,8},{8,16},{16,24},{24,0},{1,9},{9,17},{17,25},{25,1},{2,10},{10... | collective-permute-start | bytes 393224 | tf_op jit(solution)/shard_map/ppermute | solution.py:43
  114.7 4.3 %collective-permute-done.15 = bf16[1,32,2048]{2,1,0:T(8,128)(2,1)S(1)} collective-permute-done((bf16[1,32,2048]{2,1,0:T(8,128)(2,1)S(1)}, bf16[1,32,2048]{2,1,0:T(8,128)(2,1)S(1)}, u32[]{:S(2)}, u32[]{:S(2)}) %collective-permute-start.15) | collective-permute-done | bytes 131104 | tf_op jit(solution)/shard_map/ppermute | solution.py:43
  119.0 2.0 %collective-permute-done.7 = bf16[1,32,2048]{2,1,0:T(8,128)(2,1)S(1)} collective-permute-done((bf16[1,32,2048]{2,1,0:T(8,128)(2,1)S(1)}, bf16[1,32,2048]{2,1,0:T(8,128)(2,1)S(1)}, u32[]{:S(2)}, u32[]{:S(2)}) %collective-permute-start.7) | collective-permute-done | bytes 131104 | tf_op jit(solution)/shard_map/ppermute | solution.py:43
  121.0 0.7 maximum_bitcast_fusion
  (55 shorter events, 1.6 us)
Async XLA Ops:
  0.0 41.6 %copy-start = (bf16[1,1,2048,768]{3,2,1,0:T(8,128)(2,1)S(1)}, bf16[1,1,2048,768]{3,2,1,0:T(8,128)(2,1)}, u32[]{:S(2)}) copy-start(bf16[1,1,2048,768]{3,2,1,0:T(8,128)(2,1)} %param.10) | copy-start | bytes 9437188
  4.3 9.1 %copy-start.5 = (f32[1,2,32,2]{2,3,1,0:T(2,128)S(1)}, f32[1,2,32,2]{2,3,1,0:T(2,128)}, u32[]{:S(2)}) copy-start(f32[1,2,32,2]{2,3,1,0:T(2,128)} %param.8) | copy-start | bytes 1540
  4.3 9.1 %copy-start.1 = (bf16[1,2,32,2048]{3,2,1,0:T(8,128)(2,1)S(1)}, bf16[1,2,32,2048]{3,2,1,0:T(8,128)(2,1)}, u32[]{:S(2)}) copy-start(bf16[1,2,32,2048]{3,2,1,0:T(8,128)(2,1)} %param.6) | copy-start | bytes 786436
  4.3 9.1 %copy-start.4 = (f32[1,2048]{1,0:T(1,128)S(1)}, f32[1,2048]{1,0:T(1,128)}, u32[]{:S(2)}) copy-start(f32[1,2048]{1,0:T(1,128)} %param.9) | copy-start | bytes 24580
  6.6 27.4 %all-to-all-start.1 = ((bf16[8,24,1,2048]{3,1,2,0:T(8,128)(2,1)}), bf16[8,24,1,2048]{3,1,2,0:T(8,128)(2,1)}, u32[]{:S(2)}, u32[]{:S(2)}) async-start(bf16[8,24,1,2048]{3,1,2,0:T(8,128)(2,1)} %bitcast.114), calls=%async_computation.1 | async-start | bytes 1572864 | tf_op jit(solution)/shard_map/all_to_all | solution.py:101
  36.0 25.9 %all-to-all-start = ((bf16[8,24,1,2048]{3,1,2,0:T(8,128)(2,1)}), bf16[8,24,1,2048]{3,1,2,0:T(8,128)(2,1)}, u32[]{:S(2)}, u32[]{:S(2)}) async-start(bf16[8,24,1,2048]{3,1,2,0:T(8,128)(2,1)} %bitcast.113), calls=%async_computation | async-start | bytes 1572864 | tf_op jit(solution)/shard_map/all_to_all | solution.py:101
  41.7 2.0 %copy-start.6 = (bf16[1,1,384,2048]{3,2,1,0:T(8,128)(2,1)S(1)}, bf16[1,1,384,2048]{3,2,1,0:T(8,128)(2,1)}, u32[]{:S(2)}) copy-start(bf16[1,1,384,2048]{3,2,1,0:T(8,128)(2,1)} %param.11) | copy-start | bytes 4718596
  46.1 20.1 %collective-permute-start.8 = (bf16[1,24,1,2048]{3,1,0,2:T(8,128)(2,1)}, bf16[1,24,1,2048]{3,1,0,2:T(8,128)(2,1)}, u32[]{:S(2)}, u32[]{:S(2)}) collective-permute-start(bf16[1,24,1,2048]{3,1,0,2:T(8,128)(2,1)} %get-tuple-element.21), channel_id=1, source_target_pairs={{0,1},{1,0},{2,3},{3,2},{4,5},{5,4},{6,7},{7,6},{8,9},{9,8},{10,11... | collective-permute-start | bytes 294920 | tf_op jit(solution)/shard_map/ppermute | solution.py:29
  46.4 22.2 %collective-permute-start.9 = (bf16[1,24,1,2048]{3,1,0,2:T(8,128)(2,1)}, bf16[1,24,1,2048]{3,1,0,2:T(8,128)(2,1)}, u32[]{:S(2)}, u32[]{:S(2)}) collective-permute-start(bf16[1,24,1,2048]{3,1,0,2:T(8,128)(2,1)} %get-tuple-element.20), channel_id=1, source_target_pairs={{0,2},{1,3},{2,0},{3,1},{4,6},{5,7},{6,4},{7,5},{8,10},{9,11},{10,... | collective-permute-start | bytes 294920 | tf_op jit(solution)/shard_map/ppermute | solution.py:29
  48.1 23.2 %collective-permute-start.10 = (bf16[1,24,1,2048]{3,1,0,2:T(8,128)(2,1)}, bf16[1,24,1,2048]{3,1,0,2:T(8,128)(2,1)}, u32[]{:S(2)}, u32[]{:S(2)}) collective-permute-start(bf16[1,24,1,2048]{3,1,0,2:T(8,128)(2,1)} %get-tuple-element.19), channel_id=1, source_target_pairs={{0,3},{1,2},{2,1},{3,0},{4,7},{5,6},{6,5},{7,4},{8,11},{9,10},{10,... | collective-permute-start | bytes 294920 | tf_op jit(solution)/shard_map/ppermute | solution.py:29
  48.1 26.7 %collective-permute-start.11 = (bf16[1,24,1,2048]{3,1,0,2:T(8,128)(2,1)S(1)}, bf16[1,24,1,2048]{3,1,0,2:T(8,128)(2,1)}, u32[]{:S(2)}, u32[]{:S(2)}) collective-permute-start(bf16[1,24,1,2048]{3,1,0,2:T(8,128)(2,1)S(1)} %get-tuple-element.18), channel_id=1, source_target_pairs={{0,4},{1,5},{2,6},{3,7},{4,0},{5,1},{6,2},{7,3},{8,12},{9,13},{10,... | collective-permute-start | bytes 294920 | tf_op jit(solution)/shard_map/ppermute | solution.py:29
  50.7 25.6 %collective-permute-start.12 = (bf16[1,24,1,2048]{3,1,0,2:T(8,128)(2,1)S(1)}, bf16[1,24,1,2048]{3,1,0,2:T(8,128)(2,1)}, u32[]{:S(2)}, u32[]{:S(2)}) collective-permute-start(bf16[1,24,1,2048]{3,1,0,2:T(8,128)(2,1)S(1)} %get-tuple-element.17), channel_id=1, source_target_pairs={{0,5},{1,4},{2,7},{3,6},{4,1},{5,0},{6,3},{7,2},{8,13},{9,12},{10,... | collective-permute-start | bytes 294920 | tf_op jit(solution)/shard_map/ppermute | solution.py:29
  61.9 2.0 %copy-start.7 = (bf16[1,1,384,2048]{3,2,1,0:T(8,128)(2,1)S(1)}, bf16[1,1,384,2048]{3,2,1,0:T(8,128)(2,1)}, u32[]{:S(2)}) copy-start(bf16[1,1,384,2048]{3,2,1,0:T(8,128)(2,1)} %param.11) | copy-start | bytes 4718596
  66.2 13.0 %collective-permute-start.13 = (bf16[1,24,1,2048]{3,1,0,2:T(8,128)(2,1)S(1)}, bf16[1,24,1,2048]{3,1,0,2:T(8,128)(2,1)S(1)}, u32[]{:S(2)}, u32[]{:S(2)}) collective-permute-start(bf16[1,24,1,2048]{3,1,0,2:T(8,128)(2,1)S(1)} %get-tuple-element.16), channel_id=1, source_target_pairs={{0,6},{1,7},{2,4},{3,5},{4,2},{5,3},{6,0},{7,1},{8,14},{9,15},{10,... | collective-permute-start | bytes 294920 | tf_op jit(solution)/shard_map/ppermute | solution.py:29
  68.7 11.3 %collective-permute-start.14 = (bf16[1,24,1,2048]{3,1,0,2:T(8,128)(2,1)S(1)}, bf16[1,24,1,2048]{3,1,0,2:T(8,128)(2,1)S(1)}, u32[]{:S(2)}, u32[]{:S(2)}) collective-permute-start(bf16[1,24,1,2048]{3,1,0,2:T(8,128)(2,1)S(1)} %get-tuple-element.15), channel_id=1, source_target_pairs={{0,7},{1,6},{2,5},{3,4},{4,3},{5,2},{6,1},{7,0},{8,15},{9,14},{10,... | collective-permute-start | bytes 294920 | tf_op jit(solution)/shard_map/ppermute | solution.py:29
  71.3 13.5 %collective-permute-start = (bf16[1,24,1,2048]{3,1,0,2:T(8,128)(2,1)S(1)}, bf16[1,24,1,2048]{3,1,0,2:T(8,128)(2,1)S(1)}, u32[]{:S(2)}, u32[]{:S(2)}) collective-permute-start(bf16[1,24,1,2048]{3,1,0,2:T(8,128)(2,1)S(1)} %get-tuple-element.13), channel_id=1, source_target_pairs={{0,1},{1,0},{2,3},{3,2},{4,5},{5,4},{6,7},{7,6},{8,9},{9,8},{10,11... | collective-permute-start | bytes 294920 | tf_op jit(solution)/shard_map/ppermute | solution.py:29
  74.8 11.6 %collective-permute-start.1 = (bf16[1,24,1,2048]{3,1,0,2:T(8,128)(2,1)S(1)}, bf16[1,24,1,2048]{3,1,0,2:T(8,128)(2,1)S(1)}, u32[]{:S(2)}, u32[]{:S(2)}) collective-permute-start(bf16[1,24,1,2048]{3,1,0,2:T(8,128)(2,1)S(1)} %get-tuple-element.12), channel_id=1, source_target_pairs={{0,2},{1,3},{2,0},{3,1},{4,6},{5,7},{6,4},{7,5},{8,10},{9,11},{10,... | collective-permute-start | bytes 294920 | tf_op jit(solution)/shard_map/ppermute | solution.py:29
  76.3 12.9 %collective-permute-start.2 = (bf16[1,24,1,2048]{3,1,0,2:T(8,128)(2,1)S(1)}, bf16[1,24,1,2048]{3,1,0,2:T(8,128)(2,1)S(1)}, u32[]{:S(2)}, u32[]{:S(2)}) collective-permute-start(bf16[1,24,1,2048]{3,1,0,2:T(8,128)(2,1)S(1)} %get-tuple-element.11), channel_id=1, source_target_pairs={{0,3},{1,2},{2,1},{3,0},{4,7},{5,6},{6,5},{7,4},{8,11},{9,10},{10,... | collective-permute-start | bytes 294920 | tf_op jit(solution)/shard_map/ppermute | solution.py:29
  79.2 10.7 %collective-permute-start.3 = (bf16[1,24,1,2048]{3,1,0,2:T(8,128)(2,1)S(1)}, bf16[1,24,1,2048]{3,1,0,2:T(8,128)(2,1)S(1)}, u32[]{:S(2)}, u32[]{:S(2)}) collective-permute-start(bf16[1,24,1,2048]{3,1,0,2:T(8,128)(2,1)S(1)} %get-tuple-element.10), channel_id=1, source_target_pairs={{0,4},{1,5},{2,6},{3,7},{4,0},{5,1},{6,2},{7,3},{8,12},{9,13},{10,... | collective-permute-start | bytes 294920 | tf_op jit(solution)/shard_map/ppermute | solution.py:29
  80.0 15.6 %collective-permute-start.4 = (bf16[1,24,1,2048]{3,1,0,2:T(8,128)(2,1)S(1)}, bf16[1,24,1,2048]{3,1,0,2:T(8,128)(2,1)S(1)}, u32[]{:S(2)}, u32[]{:S(2)}) collective-permute-start(bf16[1,24,1,2048]{3,1,0,2:T(8,128)(2,1)S(1)} %get-tuple-element.9), channel_id=1, source_target_pairs={{0,5},{1,4},{2,7},{3,6},{4,1},{5,0},{6,3},{7,2},{8,13},{9,12},{10,... | collective-permute-start | bytes 294920 | tf_op jit(solution)/shard_map/ppermute | solution.py:29
  84.8 11.4 %collective-permute-start.5 = (bf16[1,24,1,2048]{3,1,0,2:T(8,128)(2,1)S(1)}, bf16[1,24,1,2048]{3,1,0,2:T(8,128)(2,1)S(1)}, u32[]{:S(2)}, u32[]{:S(2)}) collective-permute-start(bf16[1,24,1,2048]{3,1,0,2:T(8,128)(2,1)S(1)} %get-tuple-element.8), channel_id=1, source_target_pairs={{0,6},{1,7},{2,4},{3,5},{4,2},{5,3},{6,0},{7,1},{8,14},{9,15},{10,... | collective-permute-start | bytes 294920 | tf_op jit(solution)/shard_map/ppermute | solution.py:29
  86.4 14.7 %collective-permute-start.6 = (bf16[1,24,1,2048]{3,1,0,2:T(8,128)(2,1)}, bf16[1,24,1,2048]{3,1,0,2:T(8,128)(2,1)}, u32[]{:S(2)}, u32[]{:S(2)}) collective-permute-start(bf16[1,24,1,2048]{3,1,0,2:T(8,128)(2,1)} %get-tuple-element.7), channel_id=1, source_target_pairs={{0,7},{1,6},{2,5},{3,4},{4,3},{5,2},{6,1},{7,0},{8,15},{9,14},{10,... | collective-permute-start | bytes 294920 | tf_op jit(solution)/shard_map/ppermute | solution.py:29
  105.9 3.9 %copy-start.3 = (f32[32,2]{1,0:T(8,128)S(1)}, f32[32,2]{1,0:T(8,128)}, u32[]{:S(2)}) copy-start(f32[32,2]{1,0:T(8,128)} %copy.37) | copy-start | bytes 772
  105.9 5.7 %copy-start.2 = (bf16[1,2,32,2048]{3,2,1,0:T(8,128)(2,1)S(1)}, bf16[1,2,32,2048]{3,2,1,0:T(8,128)(2,1)}, u32[]{:S(2)}) copy-start(bf16[1,2,32,2048]{3,2,1,0:T(8,128)(2,1)} %param.6) | copy-start | bytes 786436
  111.7 7.3 %collective-permute-start.15 = (bf16[1,32,2048]{2,1,0:T(8,128)(2,1)S(1)}, bf16[1,32,2048]{2,1,0:T(8,128)(2,1)S(1)}, u32[]{:S(2)}, u32[]{:S(2)}) collective-permute-start(bf16[1,32,2048]{2,1,0:T(8,128)(2,1)S(1)} %get-tuple-element.24), channel_id=1, source_target_pairs={{0,8},{8,16},{16,24},{24,0},{1,9},{9,17},{17,25},{25,1},{2,10},{10... | collective-permute-start | bytes 393224 | tf_op jit(solution)/shard_map/ppermute | solution.py:43
  113.2 7.7 %collective-permute-start.7 = (bf16[1,32,2048]{2,1,0:T(8,128)(2,1)S(1)}, bf16[1,32,2048]{2,1,0:T(8,128)(2,1)S(1)}, u32[]{:S(2)}, u32[]{:S(2)}) collective-permute-start(bf16[1,32,2048]{2,1,0:T(8,128)(2,1)S(1)} %get-tuple-element.23), channel_id=1, source_target_pairs={{0,8},{8,16},{16,24},{24,0},{1,9},{9,17},{17,25},{25,1},{2,10},{10... | collective-permute-start | bytes 393224 | tf_op jit(solution)/shard_map/ppermute | solution.py:43
